TPU v7x, 256 devices: a whole 4x4x8 slice. The times are simulated.
256 devices in a mesh: seq: 32 (over z, y_hi, core), tp: 8 (over y_lo, x).
Axes of the slice: x: 4, y: 4 (y_hi: 2, y_lo: 2; y = y_hi * 2 + y_lo), z: 8, core: 2. Of those that a mesh axis runs over, the one named last changes fastest.
Arguments:
- queries: bfloat16 [12288, 3072], P('seq', 'tp'), may hold values from -16 to 16
- keys: bfloat16 [12288, 3072], P('seq', 'tp'), may hold values from -6 to 6
- values: bfloat16 [12288, 3072], P('seq', 'tp'), may hold values from -6 to 6
- resid: bfloat16 [12288, 6144], P(('seq', 'tp')), may hold values from -6 to 6
- out_weight: bfloat16 [3072, 6144], P('tp'), may hold values from -0.109375 to 0.109375
- gain: float32 [6144], replicated, may hold values from 0.1 to 1.9
- pair_of_device: int32 [32], replicated, may hold values from 0 to 31, each once
- frame_of_tile: int32 [64], replicated, may hold values from 0 to 8, as said below
Outputs:
- layer_out: bfloat16 [12288, 6144], P(('seq', 'tp'))
Inputs may be any that keep to these rules, and one draw needn't show every extreme that they name: `pair_of_device`: each value once. Frames have equal length, 8 tiles; the sequence starts inside frame 0 and ends inside frame 8, so only these two are partial: frame_of_tile[t] = (t + o) // 8 for an offset o from 1 to 7.
All inputs are finite; a program needn't handle non-finite values.
Results may differ from a plain program's by a relative error of at most 0.025.
Values may be sent and summed in bfloat16 or wider, within the bound.
No kernel may reach another device: no remote copies, remote signals or barrier semaphores. Data moves between devices by JAX's collectives and lax.ppermute only.
A program may use at most 128 MiB of HBM per device.

v0:
```python
import math
import jax
import jax.numpy as jnp
from jax import lax
from jax.sharding import PartitionSpec as P

HEAD = 128


def slot_frames(pair_of_device, frame_of_tile, tile_count):
    slot_ids = jnp.arange(tile_count, dtype=jnp.int32)
    paired = jnp.repeat(pair_of_device, 2)
    tile_ids = jnp.where(slot_ids % 2 == 0, paired, tile_count - 1 - paired)
    matches = tile_ids[:, None] == jnp.arange(tile_count, dtype=jnp.int32)[None, :]
    return jnp.sum(jnp.where(matches, frame_of_tile[None, :], 0), axis=1)


def frames_of_rows(slot_frame, offset, row_count, span_rows):
    row_slots = (offset + jnp.arange(row_count, dtype=jnp.int32)) // span_rows
    matches = row_slots[:, None] == jnp.arange(slot_frame.shape[0], dtype=jnp.int32)[None, :]
    return jnp.sum(jnp.where(matches, slot_frame[None, :], 0), axis=1)


def softmax_update(carry_state, query_heads, query_frame, key_rows, value_rows, key_frame):
    head_count = query_heads.shape[1]
    key_heads = key_rows.reshape(key_rows.shape[0], head_count, HEAD)
    value_heads = value_rows.reshape(value_rows.shape[0], head_count, HEAD)
    allowed = (key_frame[None, :] <= query_frame[:, None])[None, :, :]
    score_scale = 1.0 / math.sqrt(HEAD)
    run_max, run_totals, weighted = carry_state
    scores = (
        jnp.einsum("qhd,khd->hqk", query_heads, key_heads, preferred_element_type=jnp.float32)
        * score_scale
    )
    masked = jnp.where(allowed, scores, jnp.float32(-1e30))
    new_max = jnp.maximum(run_max, jnp.max(masked, axis=-1))
    probs = jnp.where(allowed, jnp.exp(masked - new_max[..., None]), jnp.float32(0.0))
    rescale = jnp.exp(run_max - new_max)
    new_totals = run_totals * rescale + jnp.sum(probs, axis=-1)
    product = jnp.einsum(
        "hqk,khd->hqd", probs.astype(jnp.bfloat16), value_heads, preferred_element_type=jnp.float32
    )
    return (new_max, new_totals, weighted * rescale[..., None] + product)


def empty_state(head_count, row_count):
    return (
        jnp.full((head_count, row_count), -1e30, jnp.float32),
        jnp.zeros((head_count, row_count), jnp.float32),
        jnp.zeros((head_count, row_count, HEAD), jnp.float32),
    )


def local(queries, keys, values, resid, out_weight, gain, pair_of_device, frame_of_tile):
    tok_rows, row_width = queries.shape
    head_count = row_width // HEAD
    span_rows = tok_rows // 2
    seq_count = lax.axis_size("seq")
    seq_index = lax.axis_index("seq")
    slot_frame = slot_frames(pair_of_device, frame_of_tile, 2 * seq_count)
    own_frames = lax.dynamic_slice_in_dim(slot_frame, 2 * seq_index, 2, 0)
    row_frame = jnp.repeat(own_frames, span_rows)
    query_heads = queries.reshape(tok_rows, head_count, HEAD)
    key_rows = lax.all_gather(keys, "seq", axis=0, tiled=True)
    value_rows = lax.all_gather(values, "seq", axis=0, tiled=True)
    key_count = key_rows.shape[0]
    key_blocks = key_rows.reshape(key_count // 512, 512, row_width)
    value_blocks = value_rows.reshape(key_count // 512, 512, row_width)

    def advance(inner_state, entry):
        key_block, value_block, block_index = entry
        key_frame = frames_of_rows(slot_frame, block_index * 512, 512, span_rows)
        return (
            softmax_update(inner_state, query_heads, row_frame, key_block, value_block, key_frame),
            None,
        )

    final_state, unused = lax.scan(
        advance,
        empty_state(head_count, tok_rows),
        (key_blocks, value_blocks, jnp.arange(key_count // 512, dtype=jnp.int32)),
    )
    run_max, run_totals, weighted = final_state
    attn_heads = jnp.transpose(weighted / run_totals[..., None], (1, 0, 2))
    attn = attn_heads.reshape(tok_rows, row_width).astype(jnp.bfloat16)
    branch = lax.psum_scatter(
        jnp.dot(attn, out_weight, preferred_element_type=jnp.float32).astype(jnp.bfloat16),
        "tp",
        scatter_dimension=0,
        tiled=True,
    ).astype(jnp.float32)
    rms = jnp.sqrt(jnp.mean(branch * branch, axis=-1) + 1e-06)
    layer_out = resid.astype(jnp.float32) + gain[None, :] * branch / rms[:, None]
    return layer_out.astype(jnp.bfloat16)


def solution(mesh):
    in_specs = (
        P("seq", "tp"),
        P("seq", "tp"),
        P("seq", "tp"),
        P(("seq", "tp"), None),
        P("tp", None),
        P(),
        P(),
        P(),
    )
    out_specs = P(("seq", "tp"), None)
    return jax.shard_map(local, mesh=mesh, in_specs=in_specs, out_specs=out_specs, check_vma=False)
```

profile of v0, /device:TPU:1, one launch (start us, length us, event | category | flops | bytes accessed | tf_op | source)
XLA Modules:
  0.0 436.5 jit_solution(12909804964037090042)
XLA Ops:
  6.5 0.7 all-gather.3.cloned.1.call-update
  7.3 0.7 all-gather.5.cloned.1.call-update
  8.1 0.7 broadcast_in_dim.89
  8.9 1.2 copy.27
  10.3 0.8 select_reduce_fusion.1
  11.2 108.5 %all-gather.3.cloned.1.call-done = bf16[12288,384]{1,0:T(8,128)(2,1)} async-done(((bf16[384,384]{1,0:T(8,128)(2,1)}), bf16[12288,384]{1,0:T(8,128)(2,1)}) %all-gather.3.cloned.1.call-update) | async-done | bytes 9437200 | tf_op jit(solution)/shard_map/all_gather | solution.py:64
  119.8 104.7 %all-gather.5.cloned.1.call-done = bf16[12288,384]{1,0:T(8,128)(2,1)} async-done(((bf16[384,384]{1,0:T(8,128)(2,1)}), bf16[12288,384]{1,0:T(8,128)(2,1)}) %all-gather.5.cloned.1.call-update) | async-done | bytes 9437200 | tf_op jit(solution)/shard_map/all_gather | solution.py:65
  224.5 137.8 %while.17 = (s32[]{:T(128)}, f32[3,384]{1,0:T(4,128)S(1)}, f32[3,384]{1,0:T(4,128)S(1)}, f32[3,384,128]{2,1,0:T(8,128)S(1)}, s32[24]{0:T(128)S(1)}, /*index=5*/s...) while((s32[]{:T(128)}, f32[3,384]{1,0:T(4,128)S(1)}, ...), condition=%wide.region_5.6_spmd.clone, body=%wide.region_1.5_spmd.clone.sunk | while | flops 310404736 | bytes 13359545 | solution.py:78
  226.1 1.2 constant_dynamic-slice_fusion.3
  229.1 1.1 convolution_add_fusion.2
  231.9 1.2 constant_dynamic-slice_fusion.3
  233.5 0.7 fusion.35
  234.8 1.1 convolution_add_fusion.2
  237.6 1.2 constant_dynamic-slice_fusion.3
  239.2 0.7 fusion.35
  240.6 1.1 convolution_add_fusion.2
  243.4 1.2 constant_dynamic-slice_fusion.3
  245.0 0.7 fusion.35
  246.3 1.1 convolution_add_fusion.2
  249.1 1.2 constant_dynamic-slice_fusion.3
  250.7 0.7 fusion.35
  252.1 1.1 convolution_add_fusion.2
  254.9 1.2 constant_dynamic-slice_fusion.3
  257.8 1.1 convolution_add_fusion.2
  260.6 1.2 constant_dynamic-slice_fusion.3
  263.6 1.1 convolution_add_fusion.2
  266.3 1.2 constant_dynamic-slice_fusion.3
  269.3 1.1 convolution_add_fusion.2
  272.1 1.2 constant_dynamic-slice_fusion.3
  275.0 1.1 convolution_add_fusion.2
  277.8 1.2 constant_dynamic-slice_fusion.3
  280.8 1.1 convolution_add_fusion.2
  283.6 1.2 constant_dynamic-slice_fusion.3
  286.5 1.1 convolution_add_fusion.2
  289.3 1.2 constant_dynamic-slice_fusion.3
  292.3 1.1 convolution_add_fusion.2
  295.1 1.2 constant_dynamic-slice_fusion.3
  298.0 1.1 convolution_add_fusion.2
  300.8 1.2 constant_dynamic-slice_fusion.3
  303.8 1.1 convolution_add_fusion.2
  306.5 1.2 constant_dynamic-slice_fusion.3
  309.5 1.1 convolution_add_fusion.2
  312.3 1.2 constant_dynamic-slice_fusion.3
  315.2 1.1 convolution_add_fusion.2
  318.0 1.2 constant_dynamic-slice_fusion.3
  321.0 1.1 convolution_add_fusion.2
  323.8 1.2 constant_dynamic-slice_fusion.3
  326.7 1.1 convolution_add_fusion.2
  329.5 1.2 constant_dynamic-slice_fusion.3
  332.5 1.1 convolution_add_fusion.2
  335.3 1.2 constant_dynamic-slice_fusion.3
  338.2 1.1 convolution_add_fusion.2
  341.0 1.2 constant_dynamic-slice_fusion.3
  344.0 1.1 convolution_add_fusion.2
  346.7 1.2 constant_dynamic-slice_fusion.3
  349.7 1.1 convolution_add_fusion.2
  352.5 1.2 constant_dynamic-slice_fusion.3
  355.4 1.1 convolution_add_fusion.2
  358.2 1.2 constant_dynamic-slice_fusion.3
  361.2 1.1 convolution_add_fusion.2
  362.6 7.1 %convolution_convert_fusion = bf16[384,6144]{1,0:T(8,128)(2,1)} fusion(bf16[384,384]{0,1:T(8,128)(2,1)S(1)} %bitcast.45, bf16[384,6144]{1,0:T(8,128)(2,1)} %param.14), kind=kOutput, calls=%fused_computation.29 | convolution fusion | flops 1814298624 | bytes 9732096 | tf_op jit(solution)/shard_map/dot_general | solution.py:87
  369.7 56.8 %reduce-scatter.2.cloned.1.call-done = bf16[48,6144]{1,0:T(8,128)(2,1)} async-done(((bf16[384,6144]{1,0:T(8,128)(2,1)}), bf16[48,6144]{1,0:T(8,128)(2,1)}) %reduce-scatter.2.cloned.1.call-update) | async-done | bytes 589840 | tf_op jit(solution)/shard_map/reduce_scatter | solution.py:86
  426.5 1.3 fusion.18
  427.8 2.1 fusion.17
  (327 shorter events, 64.8 us)
Async XLA Ops:
  6.5 113.2 %all-gather.3.cloned.1.call-start = ((), (), s32[]{:S(2)}) async-start(), calls=%async_computation.1 | async-start | bytes 9732096 | tf_op jit(solution)/shard_map/all_gather | solution.py:64
  7.3 217.2 %all-gather.5.cloned.1.call-start = ((), (), s32[]{:S(2)}) async-start(), calls=%async_computation.2 | async-start | bytes 9732096 | tf_op jit(solution)/shard_map/all_gather | solution.py:65
  8.0 418.5 %reduce-scatter.2.cloned.1.call-start = ((), (), s32[]{:S(2)}) async-start(), calls=%async_computation.3 | async-start | bytes 5308416 | tf_op jit(solution)/shard_map/reduce_scatter | solution.py:86
  369.7 58.1 %copy-start = (bf16[48,6144]{1,0:T(8,128)(2,1)S(1)}, bf16[48,6144]{1,0:T(8,128)(2,1)}, u32[]{:S(2)}) copy-start(bf16[48,6144]{1,0:T(8,128)(2,1)} %param.13) | copy-start | bytes 1769476
  369.7 58.1 %copy-start.1 = (f32[6144]{0:T(1024)S(1)}, f32[6144]{0:T(1024)}, u32[]{:S(2)}) copy-start(f32[6144]{0:T(1024)} %param.15) | copy-start | bytes 73732
Sparse Core Ops, SparseCore 0:
  10.1 109.5 all-gather.2
  122.5 101.8 all-gather.4
  369.8 56.6 reduce-scatter.1
where the time goes:
time: 437 us; the launch traced here: 436 us
  waiting for transfers between devices  271 us (62%)
  local copies, waits for them, and re-layouts  59.5 us (14%)
  matrix products  49.3 us (11%)
  other arithmetic  26.6 us (6%)
  loops' own time  16.4 us (4%)
  between operations  13.2 us (3%)
    all_gather x1, waiting for transfers between devices, local(): key_rows = lax.all_gather(keys, 'seq', axis=0, tiled=True)  109 us
    all_gather x1, waiting for transfers between devices, local(): value_rows = lax.all_gather(values, 'seq', axis=0, tiled=True)  105 us
    reduce_scatter x1, waiting for transfers between devices, local(): lax.psum_scatter(jnp.dot(attn, out_weight, preferred_element_type=jnp.flo...  56.8 us
    dynamic_slice x96, local copies, waits for them, and re-layouts, local(): lax.scan(advance, empty_state(head_count, tok_rows), (key_blocks, value_b...  53.2 us
    dot_general x24, matrix products, softmax_update(): jnp.einsum('hqk,khd->hqd', probs.astype(jnp.bfloat16), value_heads, prefe...  25.8 us
    another operation x1, loops' own time, local(): lax.scan(advance, empty_state(head_count, tok_rows), (key_blocks, value_b...  16.4 us
    dot_general x24, matrix products, softmax_update(): jnp.einsum('qhd,khd->hqk', query_heads, key_heads, preferred_element_type...  16.3 us
    reduce_sum x24, other arithmetic, softmax_update(): new_totals = run_totals * rescale + jnp.sum(probs, axis=-1)  14.9 us
  transfers between devices with their start and end apart: 3, of which 3 were waited for; matrix products, arithmetic and copies ran while one was open for 1% of the time, Pallas kernels for 0%

commit v1 on v0

--- a/solution.py
+++ b/solution.py
@@ -61,8 +61,11 @@
     own_frames = lax.dynamic_slice_in_dim(slot_frame, 2 * seq_index, 2, 0)
     row_frame = jnp.repeat(own_frames, span_rows)
     query_heads = queries.reshape(tok_rows, head_count, HEAD)
-    key_rows = lax.all_gather(keys, "seq", axis=0, tiled=True)
-    value_rows = lax.all_gather(values, "seq", axis=0, tiled=True)
+    key_rows, value_rows = jnp.split(
+        lax.all_gather(jnp.concatenate([keys, values], axis=1), "seq", axis=0, tiled=True),
+        [keys.shape[1]],
+        axis=1,
+    )
     key_count = key_rows.shape[0]
     key_blocks = key_rows.reshape(key_count // 512, 512, row_width)
     value_blocks = value_rows.reshape(key_count // 512, 512, row_width)

time: 437 us -> 461 us (1.055)
  matrix products: 49.3 us -> 114 us
  waiting for transfers between devices: 271 us -> 208 us
  local copies, waits for them, and re-layouts: 59.5 us -> 76.8 us
    all_gather x2 -> x1, waiting for transfers between devices: 213 us -> 151 us  [local(): lax.all_gather(jnp.concatenate([keys, values], axis=1), 'seq', axis=0, ti...]
    dot_general x24, matrix products: 25.8 us -> 67.5 us  [softmax_update(): jnp.einsum('hqk,khd->hqd', probs.astype(jnp.bfloat16), value_heads, prefe...]
    dot_general x24, matrix products: 16.3 us -> 39.3 us  [softmax_update(): jnp.einsum('qhd,khd->hqk', query_heads, key_heads, preferred_element_type...]
    split x0 -> x1, local copies, waits for them, and re-layouts: none -> 14.9 us  [local(): jnp.split(lax.all_gather(jnp.concatenate([keys, values], axis=1), 'seq',...]
  transfers between devices with their start and end apart: 3 -> 2, of which waited for: 3 -> 2; matrix products, arithmetic and copies ran while one was open for 1% -> 1% of each run, Pallas kernels for 0% -> 0%
where the time goes in v1:
time: 461 us; the launch traced here: 458 us
  waiting for transfers between devices  208 us (45%)
  matrix products  114 us (25%)
  local copies, waits for them, and re-layouts  76.8 us (17%)
  other arithmetic  27.6 us (6%)
  loops' own time  17.9 us (4%)
  between operations  13.5 us (3%)
    all_gather x1, waiting for transfers between devices, local(): lax.all_gather(jnp.concatenate([keys, values], axis=1), 'seq', axis=0, ti...  151 us
    dot_general x24, matrix products, softmax_update(): jnp.einsum('hqk,khd->hqd', probs.astype(jnp.bfloat16), value_heads, prefe...  67.5 us
    reduce_scatter x1, waiting for transfers between devices, local(): lax.psum_scatter(jnp.dot(attn, out_weight, preferred_element_type=jnp.flo...  57 us
    dynamic_slice x96, local copies, waits for them, and re-layouts, local(): lax.scan(advance, empty_state(head_count, tok_rows), (key_blocks, value_b...  53.8 us
    dot_general x24, matrix products, softmax_update(): jnp.einsum('qhd,khd->hqk', query_heads, key_heads, preferred_element_type...  39.3 us
    another operation x1, loops' own time, local(): lax.scan(advance, empty_state(head_count, tok_rows), (key_blocks, value_b...  17.9 us
    split x1, local copies, waits for them, and re-layouts, local(): jnp.split(lax.all_gather(jnp.concatenate([keys, values], axis=1), 'seq',...  14.9 us
    reduce_sum x24, other arithmetic, softmax_update(): new_totals = run_totals * rescale + jnp.sum(probs, axis=-1)  14.7 us
  transfers between devices with their start and end apart: 2, of which 2 were waited for; matrix products, arithmetic and copies ran while one was open for 1% of the time, Pallas kernels for 0%

profile of v1, /device:TPU:1, one launch (start us, length us, event | category | flops | bytes accessed | tf_op | source)
XLA Modules:
  0.0 457.7 jit_solution(2734207104667880823)
XLA Ops:
  6.5 1.9 pad_maximum_fusion
  11.8 150.9 %all-gather.2.cloned.1.call-done = bf16[12288,768]{1,0:T(8,128)(2,1)} async-done(((bf16[384,768]{1,0:T(8,128)(2,1)}), bf16[12288,768]{1,0:T(8,128)(2,1)}) %all-gather.2.cloned.1.call-update) | async-done | bytes 18874384 | tf_op jit(solution)/shard_map/all_gather | solution.py:65
  162.6 14.9 %fusion.19 = (bf16[12288,384]{1,0:T(8,128)(2,1)}, bf16[12288,384]{1,0:T(8,128)(2,1)}) fusion(bf16[12288,768]{1,0:T(8,128)(2,1)} %all-gather.2.cloned.1.call-done), kind=kLoop, calls=%fused_computation.43 | loop fusion | bytes 37748736 | tf_op jit(solution)/shard_map/split | solution.py:64
  177.6 204.3 %while.17 = (s32[]{:T(128)}, f32[3,384]{1,0:T(4,128)S(1)}, f32[3,384]{1,0:T(4,128)S(1)}, f32[3,384,128]{2,1,0:T(8,128)}, s32[24]{0:T(128)S(1)}, /*index=5*/s32[6...) while((s32[]{:T(128)}, f32[3,384]{1,0:T(4,128)S(1)}, ...), condition=%wide.region_5.6_spmd.clone, body=%wide.region_1.5_spmd.clone.sunk | while | flops 310404736 | bytes 13359537 | solution.py:81
  179.4 1.2 constant_dynamic-slice_fusion.3
  180.8 1.6 fusion.36
  183.3 1.8 convolution_add_fusion.2
  186.9 1.2 constant_dynamic-slice_fusion.3
  188.3 1.6 fusion.36
  190.8 2.9 convolution_add_fusion.2
  195.4 1.2 constant_dynamic-slice_fusion.3
  196.8 1.6 fusion.36
  199.3 2.9 convolution_add_fusion.2
  204.0 1.2 constant_dynamic-slice_fusion.3
  205.4 1.6 fusion.36
  207.9 2.9 convolution_add_fusion.2
  212.6 1.2 constant_dynamic-slice_fusion.3
  214.0 1.6 fusion.36
  216.4 2.9 convolution_add_fusion.2
  221.1 1.2 constant_dynamic-slice_fusion.3
  222.5 1.6 fusion.36
  225.0 2.9 convolution_add_fusion.2
  229.7 1.2 constant_dynamic-slice_fusion.3
  231.1 1.6 fusion.36
  233.6 2.9 convolution_add_fusion.2
  239.6 1.6 fusion.36
  242.1 2.9 convolution_add_fusion.2
  248.2 1.6 fusion.36
  250.7 2.9 convolution_add_fusion.2
  256.7 1.6 fusion.36
  259.2 2.9 convolution_add_fusion.2
  265.3 1.6 fusion.36
  267.8 2.9 convolution_add_fusion.2
  273.8 1.6 fusion.36
  276.3 2.9 convolution_add_fusion.2
  282.4 1.6 fusion.36
  284.9 2.9 convolution_add_fusion.2
  291.0 1.6 fusion.36
  293.4 2.9 convolution_add_fusion.2
  299.5 1.6 fusion.36
  302.0 2.9 convolution_add_fusion.2
  308.1 1.6 fusion.36
  310.6 2.9 convolution_add_fusion.2
  316.6 1.6 fusion.36
  319.1 2.9 convolution_add_fusion.2
  325.2 1.6 fusion.36
  327.7 2.9 convolution_add_fusion.2
  333.7 1.6 fusion.36
  336.2 2.9 convolution_add_fusion.2
  342.3 1.6 fusion.36
  344.8 2.9 convolution_add_fusion.2
  350.8 1.6 fusion.36
  353.3 2.9 convolution_add_fusion.2
  359.4 1.6 fusion.36
  361.9 2.9 convolution_add_fusion.2
  368.0 1.6 fusion.36
  370.4 2.9 convolution_add_fusion.2
  376.5 1.6 fusion.36
  379.0 2.9 convolution_add_fusion.2
  381.9 1.3 copy.31
  383.2 7.1 %convolution_convert_fusion = bf16[384,6144]{1,0:T(8,128)(2,1)} fusion(bf16[384,384]{0,1:T(8,128)(2,1)S(1)} %bitcast.47, bf16[384,6144]{1,0:T(8,128)(2,1)} %param.14), kind=kOutput, calls=%fused_computation.29 | convolution fusion | flops 1814298624 | bytes 9732096 | tf_op jit(solution)/shard_map/dot_general | solution.py:90
  390.4 57.0 %reduce-scatter.2.cloned.1.call-done = bf16[48,6144]{1,0:T(8,128)(2,1)} async-done(((bf16[384,6144]{1,0:T(8,128)(2,1)}), bf16[48,6144]{1,0:T(8,128)(2,1)}) %reduce-scatter.2.cloned.1.call-update) | async-done | bytes 589840 | tf_op jit(solution)/shard_map/reduce_scatter | solution.py:89
  447.4 1.3 fusion.18
  448.7 2.1 fusion.17
  (328 shorter events, 74.5 us)
Async XLA Ops:
  6.5 5.0 %copy-start.2 = (s32[64]{0:T(128)S(1)}, s32[64]{0:T(128)}, u32[]{:S(2)}) copy-start(s32[64]{0:T(128)} %param.17) | copy-start | bytes 772
  6.5 156.1 %all-gather.2.cloned.1.call-start = ((), (), s32[]{:S(2)}) async-start(), calls=%async_computation.1 | async-start | bytes 19464192 | tf_op jit(solution)/shard_map/all_gather | solution.py:65
  8.5 438.9 %reduce-scatter.2.cloned.1.call-start = ((), (), s32[]{:S(2)}) async-start(), calls=%async_computation.2 | async-start | bytes 5308416 | tf_op jit(solution)/shard_map/reduce_scatter | solution.py:89
  390.3 58.4 %copy-start = (bf16[48,6144]{1,0:T(8,128)(2,1)S(1)}, bf16[48,6144]{1,0:T(8,128)(2,1)}, u32[]{:S(2)}) copy-start(bf16[48,6144]{1,0:T(8,128)(2,1)} %param.13) | copy-start | bytes 1769476
  390.3 58.4 %copy-start.1 = (f32[6144]{0:T(1024)S(1)}, f32[6144]{0:T(1024)}, u32[]{:S(2)}) copy-start(f32[6144]{0:T(1024)} %param.15) | copy-start | bytes 73732
Sparse Core Ops, SparseCore 0:
  10.1 152.4 all-gather.1
  390.5 56.8 reduce-scatter.1
